TPU v7x, 32 devices: a whole 2x2x4 slice. The times are simulated.
32 devices in a mesh: sum: 8 (over z, x), mode: 4 (over y, core).
Axes of the slice: x: 2, y: 2, z: 4, core: 2. Of those that a mesh axis runs over, the one named last changes fastest.
Arguments:
- left_cores: bfloat16 [8, 512, 64, 512], P('sum', None, 'mode'), may hold values from -80 to 80, as said below
- right_cores: bfloat16 [8, 512, 64, 512], P('sum', None, 'mode'), may hold values from -6 to 6
- sketch: bfloat16 [64, 512, 512], P('mode'), may hold values from -0.03125 to 0.03125
Outputs:
- basis_core: float32 [512, 64, 512], P('sum', 'mode')
- carries: float32 [8, 512, 512], P('sum')
Inputs may be any that keep to these rules, and one draw needn't show every extreme that they name: `left_cores`: independent entries; each row (summand, left rank, mode index) has its own scale.
All inputs are finite; a program needn't handle non-finite values.
Results may differ from a plain program's by a relative error of at most 0.0035.
Values may be sent and summed in bfloat16 or wider, within the bound.
No kernel may reach another device: no remote copies, remote signals or barrier semaphores. Data moves between devices by JAX's collectives and lax.ppermute only.
A program may use at most 128 MiB of HBM per device.

v0:
```python
import math
import jax
import jax.numpy as jnp
from jax import lax
from jax.sharding import PartitionSpec as P

R_IN = 512
MODES = 64


def orthonormal(sketched, gram):
    lower = jnp.linalg.cholesky(gram)
    return lax.linalg.triangular_solve(
        lower, sketched, left_side=False, lower=True, transpose_a=True
    )


def per_device(left_cores, right_cores, sketch):
    sum_local, rows_in, mode_local, rank_width = left_cores.shape
    target = sketch.shape[2]
    flat_sketch = sketch.reshape(-1, target)
    flat_right = right_cores.reshape(sum_local * rank_width, -1)
    partial_map = jnp.dot(flat_right, flat_sketch, preferred_element_type=jnp.float32).reshape(
        sum_local, rank_width, target
    )
    mapped = lax.psum(partial_map, "mode").astype(jnp.bfloat16)
    flat_left = left_cores.reshape(sum_local, rows_in * mode_local, rank_width)
    local_sum = jnp.einsum("skr,srp->kp", flat_left, mapped, preferred_element_type=jnp.float32)
    local_sum = local_sum.reshape(rows_in, mode_local, target)
    factor = math.sqrt(R_IN * MODES)
    share = lax.psum_scatter(local_sum, "sum", scatter_dimension=0, tiled=True)
    flat_share = share.reshape(-1, target)
    gram_part = jnp.dot(flat_share.T, flat_share, precision=lax.Precision.HIGHEST)
    gram = lax.psum(gram_part, ("sum", "mode"))
    basis = orthonormal(flat_share, gram)
    block = basis.reshape(share.shape)
    rounded = block.astype(jnp.bfloat16)
    pieces = lax.all_gather(rounded, "sum", axis=0, tiled=True)
    count = pieces.shape[0]
    chosen = left_cores
    chosen = chosen.reshape(sum_local, count * mode_local, rank_width)
    partial_carry = jnp.einsum(
        "kp,skr->spr", pieces.reshape(-1, target), chosen, preferred_element_type=jnp.float32
    )
    carries = lax.psum(partial_carry, "mode")
    return (block * factor, carries)


def solution(mesh):
    in_specs = (P("sum", None, "mode", None), P("sum", None, "mode", None), P("mode", None, None))
    out_specs = (P("sum", "mode", None), P("sum", None, None))
    return jax.shard_map(
        per_device, mesh=mesh, in_specs=in_specs, out_specs=out_specs, check_vma=False
    )
```

profile of v0, /device:TPU:0, one launch (start us, length us, event | category | flops | bytes accessed | tf_op | source)
XLA Modules:
  0.0 864.9 jit_solution(7836462655036602845)
XLA Ops:
  7.2 16.4 %copy.36 = bf16[64,8,16,512]{3,1,2,0:T(8,128)(2,1)} copy(bf16[64,8,16,512]{3,2,1,0:T(8,128)(2,1)} %bitcast.87) | data formatting | bytes 16777216
  23.6 9.4 %convolution_bitcast_fusion.3 = f32[1,512,512]{2,1,0:T(8,128)S(1)} fusion(bf16[512,8192]{1,0:T(8,128)(2,1)} %bitcast.88, bf16[8192,512]{1,0:T(8,128)(2,1)} %bitcast.91), kind=kOutput, calls=%fused_computation.13 | convolution fusion | flops 4294967296 | bytes 17825792 | tf_op jit(solution)/shard_map/dot_general | solution.py:23
  33.0 28.2 %all-reduce.8 = bf16[1,512,512]{2,1,0:T(8,128)(2,1)S(1)} all-reduce(f32[1,512,512]{2,1,0:T(8,128)S(1)} %convolution_bitcast_fusion.3), channel_id=1, replica_groups=mesh['sum'=8,'mode'=4] {'mode'}, use_global_device_ids=true, to_apply=%region_0.0 | all-reduce | flops 262144 | bytes 1572864 | tf_op jit(solution)/shard_map/psum | solution.py:26
  61.2 27.3 %convolution_bitcast_fusion = f32[512,16,512]{0,2,1:T(8,128)} fusion(bf16[512,16,512]{2,1,0:T(8,128)(2,1)} %bitcast.81, bf16[1,512,512]{2,1,0:T(8,128)(2,1)S(1)} %all-reduce.8), kind=kOutput, calls=%fused_computation.2 | convolution fusion | flops 4294967296 | bytes 25690112 | tf_op jit(solution)/shard_map/skr,srp->kp/dot_general | solution.py:28
  88.6 20.2 %copy.23 = f32[512,16,512]{2,1,0:T(8,128)} copy(f32[512,16,512]{0,2,1:T(8,128)} %convolution_bitcast_fusion) | data formatting | bytes 33554432 | tf_op jit(solution)/shard_map/skr,srp->kp/dot_general | solution.py:28
  109.3 282.2 %reduce-scatter.2.cloned.1.call-done = f32[64,16,512]{2,1,0:T(8,128)} async-done(((f32[512,16,512]{2,1,0:T(8,128)}), f32[64,16,512]{2,1,0:T(8,128)}) %reduce-scatter.2.cloned.1.call-update) | async-done | bytes 2097168 | tf_op jit(solution)/shard_map/reduce_scatter | solution.py:31
  391.5 6.7 convolution_bitcast_fusion.2
  398.3 129.0 %all-reduce.5.cloned.1.call-done = f32[512,512]{0,1:T(8,128)} async-done(((f32[512,512]{0,1:T(8,128)}), f32[512,512]{0,1:T(8,128)}) %all-reduce.5.cloned.1.call-update) | async-done | bytes 1048592 | tf_op jit(solution)/shard_map/psum | solution.py:34
  527.3 1.6 copy.27
  530.2 11.7 %cholesky.104 = f32[128,128]{1,0:T(8,128)S(1)} custom-call(f32[128,128]{1,0:T(8,128)S(1)} %cholesky.266), custom_call_target="Cholesky" | custom-call | tf_op jit(solution)/shard_map/jit(cholesky)/cholesky | solution.py:12
  541.9 9.8 %custom-call.30 = f32[1,128,128]{1,2,0:T(8,128)S(1)} custom-call(f32[1,128,128]{2,1,0:T(8,128)S(1)} %get-tuple-element.31), custom_call_target="InvertDiagBlocksLowerTriangular" | custom-call | tf_op jit(solution)/shard_map/jit(cholesky)/cholesky | solution.py:12
  554.4 11.7 %cholesky.217 = f32[128,128]{1,0:T(8,128)S(1)} custom-call(f32[128,128]{1,0:T(8,128)S(1)} %cholesky.270), custom_call_target="Cholesky" | custom-call | tf_op jit(solution)/shard_map/jit(cholesky)/cholesky | solution.py:12
  566.1 10.0 %custom-call.31 = f32[1,128,128]{1,2,0:T(8,128)S(1)} custom-call(f32[1,128,128]{2,1,0:T(8,128)S(1)} %get-tuple-element.28), custom_call_target="InvertDiagBlocksLowerTriangular" | custom-call | tf_op jit(solution)/shard_map/jit(cholesky)/cholesky | solution.py:12
  577.7 11.7 %cholesky.238 = f32[128,128]{1,0:T(8,128)S(1)} custom-call(f32[128,128]{1,0:T(8,128)S(1)} %cholesky.275), custom_call_target="Cholesky" | custom-call | tf_op jit(solution)/shard_map/jit(cholesky)/cholesky | solution.py:12
  590.1 9.8 %custom-call.32 = f32[1,128,128]{1,2,0:T(8,128)S(1)} custom-call(f32[1,128,128]{2,1,0:T(8,128)S(1)} %get-tuple-element.25), custom_call_target="InvertDiagBlocksLowerTriangular" | custom-call | tf_op jit(solution)/shard_map/jit(cholesky)/cholesky | solution.py:12
  601.4 11.7 %cholesky.255 = f32[128,128]{1,0:T(8,128)S(1)} custom-call(f32[128,128]{1,0:T(8,128)S(1)} %convolution_subtract_fusion.4), custom_call_target="Cholesky" | custom-call | tf_op jit(solution)/shard_map/jit(cholesky)/cholesky | solution.py:12
  618.3 14.2 %while.1 = (s32[]{:T(128)}, f32[512,512]{1,0:T(8,128)}, s32[4,2]{0,1:T(2,128)S(1)}, f32[4,128,128]{2,1,0:T(8,128)}, s32[]{:T(128)}) while((s32[]{:T(128)}, f32[512,512]{1,0:T(8,128)}, s32[4,2]{0,1:T(2,128)S(1)}, f32[4,128,128]{2,1,0:T(8,128)}, s32[]{:T(128)}) %tuple.32), condition=%wide.while_cond, body=%wide.while_body.sunk | while | flops 2 | bytes 132705 | solution.py:13
  619.0 2.9 bitcast_dynamic-update-slice_fusion.2
  622.5 2.9 bitcast_dynamic-update-slice_fusion.2
  626.1 2.9 bitcast_dynamic-update-slice_fusion.2
  629.6 2.8 bitcast_dynamic-update-slice_fusion.2
  632.4 40.1 %custom-call.33 = f32[4,128,128]{1,2,0:T(8,128)S(1)} custom-call(f32[4,128,128]{2,1,0:T(8,128)} %get-tuple-element.9), custom_call_target="InvertDiagBlocksLowerTriangular" | custom-call | tf_op jit(solution)/shard_map/triangular_solve | solution.py:13
  673.2 1.8 convolution_subtract_fusion.1
  675.7 2.7 convolution_subtract_fusion
  679.0 3.8 fusion.7
  684.5 1.3 copy.29
  686.1 123.8 %all-gather.2.cloned.1.call-done = bf16[512,16,512]{2,1,0:T(8,128)(2,1)} async-done(((bf16[64,16,512]{2,1,0:T(8,128)(2,1)}), bf16[512,16,512]{2,1,0:T(8,128)(2,1)}) %all-gather.2.cloned.1.call-update) | async-done | bytes 8388624 | tf_op jit(solution)/shard_map/all_gather | solution.py:38
  809.9 11.2 %convolution_bitcast_fusion.1 = f32[1,512,512]{2,1,0:T(8,128)} fusion(bf16[8192,512]{1,0:T(8,128)(2,1)} %bitcast.92, bf16[8192,512]{1,0:T(8,128)(2,1)} %bitcast.82), kind=kOutput, calls=%fused_computation.11 | convolution fusion | flops 4294967296 | bytes 17825792 | tf_op jit(solution)/shard_map/kp,skr->spr/dot_general | solution.py:42
  821.2 1.5 fusion.11
  822.6 1.8 copy.28
  824.4 31.2 %all-reduce.7.cloned.1.call-done = f32[1,512,512]{2,1,0:T(8,128)} async-done(((f32[1,512,512]{2,1,0:T(8,128)}), f32[1,512,512]{2,1,0:T(8,128)}) %all-reduce.7.cloned.1.call-update) | async-done | bytes 1048592 | tf_op jit(solution)/shard_map/psum | solution.py:45
  855.6 2.3 copy.58
  (53 shorter events, 17.3 us)
Async XLA Ops:
  7.2 384.3 %reduce-scatter.2.cloned.1.call-start = ((), (), s32[]{:S(2)}) async-start(), calls=%async_computation.1 | async-start | bytes 18874368 | tf_op jit(solution)/shard_map/reduce_scatter | solution.py:31
  108.8 418.5 %all-reduce.5.cloned.1.call-start = ((), (), s32[]{:S(2)}) async-start(), calls=%async_computation.2 | async-start | bytes 2097152 | tf_op jit(solution)/shard_map/psum | solution.py:34
  398.2 411.7 %all-gather.2.cloned.1.call-start = ((), (), s32[]{:S(2)}) async-start(), calls=%async_computation.3 | async-start | bytes 9437184 | tf_op jit(solution)/shard_map/all_gather | solution.py:38
  527.3 1.7 copy-start.3
  529.2 1.0 copy-start.4
  577.6 94.9 %copy-start = (f32[64,16,512]{2,1,0:T(8,128)S(1)}, f32[64,16,512]{2,1,0:T(8,128)}, u32[]{:S(2)}) copy-start(f32[64,16,512]{2,1,0:T(8,128)} %reduce-scatter.2.cloned.1.call-done) | copy-start | bytes 6291460
  679.0 4.5 copy-start.1
  683.5 0.8 copy-start.2
  685.8 169.8 %all-reduce.7.cloned.1.call-start = ((), (), s32[]{:S(2)}) async-start(), calls=%async_computation.4 | async-start | bytes 2097152 | tf_op jit(solution)/shard_map/psum | solution.py:45
Sparse Core Ops, SparseCore 0:
  108.9 282.4 reduce-scatter.1
  398.3 128.9 all-reduce.4
  686.0 123.8 all-gather.1
  821.3 34.2 all-reduce.6
where the time goes:
time: 875 us; the launch traced here: 865 us
  waiting for transfers between devices  566 us (65%)
  other arithmetic  122 us (14%)
  matrix products  71.1 us (8%)
  local copies, waits for them, and re-layouts  59.7 us (7%)
  blocking collectives  28.2 us (3%)
  between operations  17 us (2%)
    reduce_scatter x1, waiting for transfers between devices, per_device(): share = lax.psum_scatter(local_sum, 'sum', scatter_dimension=0, tiled=True)  282 us
    psum x1, waiting for transfers between devices, per_device(): gram = lax.psum(gram_part, ('sum', 'mode'))  129 us
    all_gather x1, waiting for transfers between devices, per_device(): pieces = lax.all_gather(rounded, 'sum', axis=0, tiled=True)  124 us
    another operation x14, other arithmetic, orthonormal(): lower = jnp.linalg.cholesky(gram)  78.6 us
    another operation x3, other arithmetic, orthonormal(): lax.linalg.triangular_solve(lower, sketched, left_side=False, lower=True,...  41.4 us
    psum x1, waiting for transfers between devices, per_device(): carries = lax.psum(partial_carry, 'mode')  31.2 us
    psum x1, blocking collectives, per_device(): mapped = lax.psum(partial_map, 'mode').astype(jnp.bfloat16)  28.2 us
    dot_general x1, matrix products, per_device(): jnp.einsum('skr,srp->kp', flat_left, mapped, preferred_element_type=jnp.f...  27.3 us
  transfers between devices with their start and end apart: 4, of which 4 were waited for; matrix products, arithmetic and copies ran while one was open for 0% of the time, Pallas kernels for 0%

commit v1 on v0

--- a/solution.py
+++ b/solution.py
@@ -35,7 +35,21 @@
     basis = orthonormal(flat_share, gram)
     block = basis.reshape(share.shape)
     rounded = block.astype(jnp.bfloat16)
-    pieces = lax.all_gather(rounded, "sum", axis=0, tiled=True)
+    ways, here, step = (lax.axis_size("sum"), lax.axis_index("sum"), rounded.shape[0])
+    shape = [n * ways if d == 0 else n for d, n in enumerate(rounded.shape)]
+    full = lax.dynamic_update_slice_in_dim(
+        jnp.zeros(shape, rounded.dtype), rounded, here * step, axis=0
+    )
+    going_up = going_down = rounded
+    for far in range(1, ways // 2 + 1):
+        going_up = lax.ppermute(going_up, "sum", [(d, (d + 1) % ways) for d in range(ways)])
+        full = lax.dynamic_update_slice_in_dim(full, going_up, (here - far) % ways * step, axis=0)
+        if 2 * far < ways:
+            going_down = lax.ppermute(going_down, "sum", [(d, (d - 1) % ways) for d in range(ways)])
+            full = lax.dynamic_update_slice_in_dim(
+                full, going_down, (here + far) % ways * step, axis=0
+            )
+    pieces = full
     count = pieces.shape[0]
     chosen = left_cores
     chosen = chosen.reshape(sum_local, count * mode_local, rank_width)

time: 875 us -> 913 us (1.043)
  waiting for transfers between devices: 566 us -> 585 us
  starting transfers between devices: 0.82 us -> 17.6 us
    ppermute x0 -> x7, waiting for transfers between devices: none -> 141 us  [the longest x4 141 us: per_device(): lax.ppermute(going_up, 'sum', [(d, (d + 1) % ways) for d in range(ways)])]
    all_gather x1 -> x0, waiting for transfers between devices: 124 us -> none  [per_device(): pieces = lax.all_gather(rounded, 'sum', axis=0, tiled=True)]
    ppermute x0 -> x7, starting transfers between devices: none -> 17 us  [the longest x4 9.29 us: per_device(): lax.ppermute(going_up, 'sum', [(d, (d + 1) % ways) for d in range(ways)])]
    unnamed x12 -> x22, local copies, waits for them, and re-layouts: 20.4 us -> 20.5 us
  transfers between devices with their start and end apart: 4 -> 10, of which waited for: 4 -> 7; matrix products, arithmetic and copies ran while one was open for 0% -> 1% of each run, Pallas kernels for 0% -> 0%
where the time goes in v1:
time: 913 us; the launch traced here: 903 us
  waiting for transfers between devices  585 us (64%)
  other arithmetic  123 us (13%)
  local copies, waits for them, and re-layouts  66.1 us (7%)
  matrix products  65.3 us (7%)
  blocking collectives  28.2 us (3%)
  starting transfers between devices  17.6 us (2%)
  between operations  17.1 us (2%)
    reduce_scatter x1, waiting for transfers between devices, per_device(): share = lax.psum_scatter(local_sum, 'sum', scatter_dimension=0, tiled=True)  283 us
    ppermute x4, waiting for transfers between devices, per_device(): lax.ppermute(going_up, 'sum', [(d, (d + 1) % ways) for d in range(ways)])  141 us
    psum x1, waiting for transfers between devices, per_device(): gram = lax.psum(gram_part, ('sum', 'mode'))  129 us
    another operation x14, other arithmetic, orthonormal(): lower = jnp.linalg.cholesky(gram)  78.6 us
    another operation x3, other arithmetic, orthonormal(): lax.linalg.triangular_solve(lower, sketched, left_side=False, lower=True,...  41.4 us
    psum x1, waiting for transfers between devices, per_device(): carries = lax.psum(partial_carry, 'mode')  32.2 us
    psum x1, blocking collectives, per_device(): mapped = lax.psum(partial_map, 'mode').astype(jnp.bfloat16)  28.2 us
    dot_general x1, matrix products, per_device(): jnp.einsum('skr,srp->kp', flat_left, mapped, preferred_element_type=jnp.f...  27.3 us
  transfers between devices with their start and end apart: 10, of which 7 were waited for; matrix products, arithmetic and copies ran while one was open for 1% of the time, Pallas kernels for 0%

profile of v1, /device:TPU:0, one launch (start us, length us, event | category | flops | bytes accessed | tf_op | source)
XLA Modules:
  0.0 902.6 jit_solution(8924212241882664668)
XLA Ops:
  7.2 16.4 %copy.36 = bf16[64,8,16,512]{3,1,2,0:T(8,128)(2,1)} copy(bf16[64,8,16,512]{3,2,1,0:T(8,128)(2,1)} %bitcast.89) | data formatting | bytes 16777216
  23.6 9.4 %convolution_bitcast_fusion.3 = f32[1,512,512]{2,1,0:T(8,128)S(1)} fusion(bf16[512,8192]{1,0:T(8,128)(2,1)} %bitcast.91, bf16[8192,512]{1,0:T(8,128)(2,1)} %bitcast.96), kind=kOutput, calls=%fused_computation.13 | convolution fusion | flops 4294967296 | bytes 17825792 | tf_op jit(solution)/shard_map/dot_general | solution.py:23
  33.0 28.2 %all-reduce.8 = bf16[1,512,512]{2,1,0:T(8,128)(2,1)S(1)} all-reduce(f32[1,512,512]{2,1,0:T(8,128)S(1)} %convolution_bitcast_fusion.3), channel_id=1, replica_groups=mesh['sum'=8,'mode'=4] {'mode'}, use_global_device_ids=true, to_apply=%region_0.0 | all-reduce | flops 262144 | bytes 1572864 | tf_op jit(solution)/shard_map/psum | solution.py:26
  61.2 27.3 %convolution_bitcast_fusion = f32[512,16,512]{0,2,1:T(8,128)} fusion(bf16[512,16,512]{2,1,0:T(8,128)(2,1)} %bitcast.81, bf16[1,512,512]{2,1,0:T(8,128)(2,1)S(1)} %all-reduce.8), kind=kOutput, calls=%fused_computation.2 | convolution fusion | flops 4294967296 | bytes 25690112 | tf_op jit(solution)/shard_map/skr,srp->kp/dot_general | solution.py:28
  88.5 20.2 %copy.23 = f32[512,16,512]{2,1,0:T(8,128)} copy(f32[512,16,512]{0,2,1:T(8,128)} %convolution_bitcast_fusion) | data formatting | bytes 33554432 | tf_op jit(solution)/shard_map/skr,srp->kp/dot_general | solution.py:28
  109.2 282.8 %reduce-scatter.2.cloned.1.call-done = f32[64,16,512]{2,1,0:T(8,128)} async-done(((f32[512,16,512]{2,1,0:T(8,128)}), f32[64,16,512]{2,1,0:T(8,128)}) %reduce-scatter.2.cloned.1.call-update) | async-done | bytes 2097168 | tf_op jit(solution)/shard_map/reduce_scatter | solution.py:31
  392.1 6.8 convolution_bitcast_fusion.2
  398.9 128.9 %all-reduce.5.cloned.1.call-done = f32[512,512]{0,1:T(8,128)} async-done(((f32[512,512]{0,1:T(8,128)}), f32[512,512]{0,1:T(8,128)}) %all-reduce.5.cloned.1.call-update) | async-done | bytes 1048592 | tf_op jit(solution)/shard_map/psum | solution.py:34
  531.8 11.7 %cholesky.104 = f32[128,128]{1,0:T(8,128)S(1)} custom-call(f32[128,128]{1,0:T(8,128)S(1)} %cholesky.266), custom_call_target="Cholesky" | custom-call | tf_op jit(solution)/shard_map/jit(cholesky)/cholesky | solution.py:12
  543.5 9.8 %custom-call.30 = f32[1,128,128]{1,2,0:T(8,128)S(1)} custom-call(f32[1,128,128]{2,1,0:T(8,128)S(1)} %get-tuple-element.31), custom_call_target="InvertDiagBlocksLowerTriangular" | custom-call | tf_op jit(solution)/shard_map/jit(cholesky)/cholesky | solution.py:12
  556.0 11.7 %cholesky.217 = f32[128,128]{1,0:T(8,128)S(1)} custom-call(f32[128,128]{1,0:T(8,128)S(1)} %cholesky.270), custom_call_target="Cholesky" | custom-call | tf_op jit(solution)/shard_map/jit(cholesky)/cholesky | solution.py:12
  567.7 10.0 %custom-call.31 = f32[1,128,128]{1,2,0:T(8,128)S(1)} custom-call(f32[1,128,128]{2,1,0:T(8,128)S(1)} %get-tuple-element.28), custom_call_target="InvertDiagBlocksLowerTriangular" | custom-call | tf_op jit(solution)/shard_map/jit(cholesky)/cholesky | solution.py:12
  579.3 11.7 %cholesky.238 = f32[128,128]{1,0:T(8,128)S(1)} custom-call(f32[128,128]{1,0:T(8,128)S(1)} %cholesky.275), custom_call_target="Cholesky" | custom-call | tf_op jit(solution)/shard_map/jit(cholesky)/cholesky | solution.py:12
  591.7 9.8 %custom-call.32 = f32[1,128,128]{1,2,0:T(8,128)S(1)} custom-call(f32[1,128,128]{2,1,0:T(8,128)S(1)} %get-tuple-element.25), custom_call_target="InvertDiagBlocksLowerTriangular" | custom-call | tf_op jit(solution)/shard_map/jit(cholesky)/cholesky | solution.py:12
  602.9 11.7 %cholesky.255 = f32[128,128]{1,0:T(8,128)S(1)} custom-call(f32[128,128]{1,0:T(8,128)S(1)} %convolution_subtract_fusion.4), custom_call_target="Cholesky" | custom-call | tf_op jit(solution)/shard_map/jit(cholesky)/cholesky | solution.py:12
  619.8 13.7 %while.1 = (s32[]{:T(128)}, f32[512,512]{1,0:T(8,128)}, s32[4,2]{0,1:T(2,128)S(1)}, f32[4,128,128]{2,1,0:T(8,128)}, s32[]{:T(128)}) while((s32[]{:T(128)}, f32[512,512]{1,0:T(8,128)}, s32[4,2]{0,1:T(2,128)S(1)}, f32[4,128,128]{2,1,0:T(8,128)}, s32[]{:T(128)}) %tuple.32), condition=%wide.while_cond, body=%wide.while_body.sunk | while | flops 2 | bytes 132705 | solution.py:13
  620.5 2.8 bitcast_dynamic-update-slice_fusion.2
  623.9 2.8 bitcast_dynamic-update-slice_fusion.2
  627.3 2.8 bitcast_dynamic-update-slice_fusion.2
  630.8 2.8 bitcast_dynamic-update-slice_fusion.2
  633.5 40.1 %custom-call.33 = f32[4,128,128]{1,2,0:T(8,128)S(1)} custom-call(f32[4,128,128]{2,1,0:T(8,128)} %get-tuple-element.9), custom_call_target="InvertDiagBlocksLowerTriangular" | custom-call | tf_op jit(solution)/shard_map/triangular_solve | solution.py:13
  676.8 2.7 convolution_subtract_fusion
  680.1 3.8 fusion.7
  687.7 3.3 collective-permute-start.1
  690.9 40.8 %collective-permute-done = bf16[64,16,512]{2,1,0:T(8,128)(2,1)S(1)} collective-permute-done((bf16[64,16,512]{2,1,0:T(8,128)(2,1)S(1)}, bf16[64,16,512]{2,1,0:T(8,128)(2,1)S(1)}, u32[]{:S(2)}, u32[]{:S(2)}) %collective-permute-start) | collective-permute-done | bytes 1048608 | tf_op jit(solution)/shard_map/ppermute | solution.py:45
  736.4 41.7 %collective-permute-done.2 = bf16[64,16,512]{2,1,0:T(8,128)(2,1)S(1)} collective-permute-done((bf16[64,16,512]{2,1,0:T(8,128)(2,1)S(1)}, bf16[64,16,512]{2,1,0:T(8,128)(2,1)S(1)}, u32[]{:S(2)}, u32[]{:S(2)}) %collective-permute-start.2) | collective-permute-done | bytes 1048608 | tf_op jit(solution)/shard_map/ppermute | solution.py:45
  778.1 2.5 collective-permute-start.4
  782.9 41.8 %collective-permute-done.4 = bf16[64,16,512]{2,1,0:T(8,128)(2,1)} collective-permute-done((bf16[64,16,512]{2,1,0:T(8,128)(2,1)S(1)}, bf16[64,16,512]{2,1,0:T(8,128)(2,1)}, u32[]{:S(2)}, u32[]{:S(2)}) %collective-permute-start.4) | collective-permute-done | bytes 1048608 | tf_op jit(solution)/shard_map/ppermute | solution.py:45
  824.6 2.8 collective-permute-start.6
  833.9 17.1 %collective-permute-done.6 = bf16[64,16,512]{2,1,0:T(8,128)(2,1)} collective-permute-done((bf16[64,16,512]{2,1,0:T(8,128)(2,1)}, bf16[64,16,512]{2,1,0:T(8,128)(2,1)}, u32[]{:S(2)}, u32[]{:S(2)}) %collective-permute-start.6) | collective-permute-done | bytes 1048608 | tf_op jit(solution)/shard_map/ppermute | solution.py:45
  852.4 5.5 convolution_bitcast_fusion.1
  861.1 32.2 %all-reduce.7.cloned.1.call-done = f32[1,512,512]{2,1,0:T(8,128)} async-done(((f32[1,512,512]{2,1,0:T(8,128)}), f32[1,512,512]{2,1,0:T(8,128)}) %all-reduce.7.cloned.1.call-update) | async-done | bytes 1048592 | tf_op jit(solution)/shard_map/psum | solution.py:59
  (84 shorter events, 43.6 us)
Async XLA Ops:
  7.2 384.9 %reduce-scatter.2.cloned.1.call-start = ((), (), s32[]{:S(2)}) async-start(), calls=%async_computation.1 | async-start | bytes 18874368 | tf_op jit(solution)/shard_map/reduce_scatter | solution.py:31
  108.8 419.0 %all-reduce.5.cloned.1.call-start = ((), (), s32[]{:S(2)}) async-start(), calls=%async_computation.2 | async-start | bytes 2097152 | tf_op jit(solution)/shard_map/psum | solution.py:34
  398.8 274.9 %copy-start = (f32[64,16,512]{2,1,0:T(8,128)S(1)}, f32[64,16,512]{2,1,0:T(8,128)}, u32[]{:S(2)}) copy-start(f32[64,16,512]{2,1,0:T(8,128)} %reduce-scatter.2.cloned.1.call-done) | copy-start | bytes 6291460
  398.8 494.5 %all-reduce.7.cloned.1.call-start = ((), (), s32[]{:S(2)}) async-start(), calls=%async_computation.3 | async-start | bytes 2097152 | tf_op jit(solution)/shard_map/psum | solution.py:59
  530.8 1.0 copy-start.3
  680.1 4.5 copy-start.1
  684.6 0.8 copy-start.2
  686.1 45.5 %collective-permute-start = (bf16[64,16,512]{2,1,0:T(8,128)(2,1)S(1)}, bf16[64,16,512]{2,1,0:T(8,128)(2,1)S(1)}, u32[]{:S(2)}, u32[]{:S(2)}) collective-permute-start(bf16[64,16,512]{2,1,0:T(8,128)(2,1)S(1)} %bitcast.92), channel_id=1, source_target_pairs={{0,4},{4,8},{8,12},{12,16},{16,20},{20,24},{24,28},{28,0},{1,5},{5... | collective-permute-start | bytes 3145736 | tf_op jit(solution)/shard_map/ppermute | solution.py:45
  687.7 46.5 %collective-permute-start.1 = (bf16[64,16,512]{2,1,0:T(8,128)(2,1)S(1)}, bf16[64,16,512]{2,1,0:T(8,128)(2,1)S(1)}, u32[]{:S(2)}, u32[]{:S(2)}) collective-permute-start(bf16[64,16,512]{2,1,0:T(8,128)(2,1)S(1)} %bitcast.93), channel_id=1, source_target_pairs={{0,28},{4,0},{8,4},{12,8},{16,12},{20,16},{24,20},{28,24},{1,29},{... | collective-permute-start | bytes 3145736 | tf_op jit(solution)/shard_map/ppermute | solution.py:48
  731.7 46.4 %collective-permute-start.2 = (bf16[64,16,512]{2,1,0:T(8,128)(2,1)S(1)}, bf16[64,16,512]{2,1,0:T(8,128)(2,1)S(1)}, u32[]{:S(2)}, u32[]{:S(2)}) collective-permute-start(bf16[64,16,512]{2,1,0:T(8,128)(2,1)S(1)} %collective-permute-done), channel_id=1, source_target_pairs={{0,4},{4,8},{8,12},{12,16},{16,20},{20,24},{24,28},{28,0},{1,5},{5... | collective-permute-start | bytes 3145736 | tf_op jit(solution)/shard_map/ppermute | solution.py:45
  734.2 44.0 %copy-start.4 = (bf16[64,16,512]{2,1,0:T(8,128)(2,1)}, bf16[64,16,512]{2,1,0:T(8,128)(2,1)S(1)}, u32[]{:S(2)}) copy-start(bf16[64,16,512]{2,1,0:T(8,128)(2,1)S(1)} %collective-permute-done.1) | copy-start | bytes 3145732
  734.2 46.4 %collective-permute-start.3 = (bf16[64,16,512]{2,1,0:T(8,128)(2,1)S(1)}, bf16[64,16,512]{2,1,0:T(8,128)(2,1)}, u32[]{:S(2)}, u32[]{:S(2)}) collective-permute-start(bf16[64,16,512]{2,1,0:T(8,128)(2,1)S(1)} %collective-permute-done.1), channel_id=1, source_target_pairs={{0,28},{4,0},{8,4},{12,8},{16,12},{20,16},{24,20},{28,24},{1,29},{... | collective-permute-start | bytes 3145736 | tf_op jit(solution)/shard_map/ppermute | solution.py:48
  778.1 2.5 copy-start.6
  778.1 46.5 %collective-permute-start.4 = (bf16[64,16,512]{2,1,0:T(8,128)(2,1)S(1)}, bf16[64,16,512]{2,1,0:T(8,128)(2,1)}, u32[]{:S(2)}, u32[]{:S(2)}) collective-permute-start(bf16[64,16,512]{2,1,0:T(8,128)(2,1)S(1)} %collective-permute-done.2), channel_id=1, source_target_pairs={{0,4},{4,8},{8,12},{12,16},{16,20},{20,24},{24,28},{28,0},{1,5},{5... | collective-permute-start | bytes 3145736 | tf_op jit(solution)/shard_map/ppermute | solution.py:45
  780.6 52.0 %collective-permute-start.5 = (bf16[64,16,512]{2,1,0:T(8,128)(2,1)}, bf16[64,16,512]{2,1,0:T(8,128)(2,1)}, u32[]{:S(2)}, u32[]{:S(2)}) collective-permute-start(bf16[64,16,512]{2,1,0:T(8,128)(2,1)} %collective-permute-done.3), channel_id=1, source_target_pairs={{0,28},{4,0},{8,4},{12,8},{16,12},{20,16},{24,20},{28,24},{1,29},{... | collective-permute-start | bytes 3145736 | tf_op jit(solution)/shard_map/ppermute | solution.py:48
  824.6 26.4 %collective-permute-start.6 = (bf16[64,16,512]{2,1,0:T(8,128)(2,1)}, bf16[64,16,512]{2,1,0:T(8,128)(2,1)}, u32[]{:S(2)}, u32[]{:S(2)}) collective-permute-start(bf16[64,16,512]{2,1,0:T(8,128)(2,1)} %collective-permute-done.4), channel_id=1, source_target_pairs={{0,4},{4,8},{8,12},{12,16},{16,20},{20,24},{24,28},{28,0},{1,5},{5... | collective-permute-start | bytes 3145736 | tf_op jit(solution)/shard_map/ppermute | solution.py:45
  827.5 1.3 copy-start.5
  827.5 1.5 copy-start.7
  828.5 23.8 %slice-start = ((s8[8388608]{0:T(1024)(128)(4,1)}), s8[4194304]{0:T(1024)(128)(4,1)S(1)}, s32[]{:S(2)}) async-start(s8[8388608]{0:T(1024)(128)(4,1)} %bitcast.82), calls=%async_computation.4 | async-start | bytes 8388608
  829.1 23.2 %slice-start.1 = ((s8[8388608]{0:T(1024)(128)(4,1)}), s8[4194304]{0:T(1024)(128)(4,1)S(1)}, s32[]{:S(2)}) async-start(s8[8388608]{0:T(1024)(128)(4,1)} %bitcast.82), calls=%async_computation.5 | async-start | bytes 8388608
Sparse Core Ops, SparseCore 0:
  108.9 283.1 reduce-scatter.1
  399.0 128.7 all-reduce.4
  858.0 35.2 all-reduce.6
